TPU v7x, 32 devices: a whole 2x2x4 slice. The times are simulated.
32 devices in a mesh: vol: 8 (over z, y), ptcl: 4 (over x, core).
Axes of the slice: x: 2, y: 2, z: 4, core: 2. Of those that a mesh axis runs over, the one named last changes fastest.
Arguments:
- images: bfloat16 [32, 256, 256], P(('vol', 'ptcl')), may hold values from -6 to 6
- defocus: bfloat16 [32], P(('vol', 'ptcl')), may hold values from 20 to 200
- volume: float32 [4096, 256], P('vol'), may hold values from -6 to 6
- counts: int32 [8, 4, 8], P('vol', 'ptcl'), may hold values from 1 to 96, as said below
- slot_pixel: int32 [8, 4, 8, 96], P('vol', 'ptcl'), may hold values from 0 to 511, as said below
- slot_taps: int32 [8, 4, 8, 8, 96], P('vol', 'ptcl'), may hold values from 0 to 511, as said below
- slot_weights: bfloat16 [8, 4, 8, 8, 96], P('vol', 'ptcl'), may hold values from 0.019897461 to 0.25
Outputs:
- volume_next: float32 [4096, 256], P('vol')
Inputs may be any that keep to these rules, and one draw needn't show every extreme that they name: The 8 counts of each holder sum to 512; in each particle shard one owner receives exactly 96 live slots from every holder of that shard. `slot_pixel`: the live slots of a holder (slot index below its count) name each of its 512 pixel blocks exactly once; the other slots hold valid ids. `slot_taps`: the 8 taps of one slot name 8 different blocks.
All inputs are finite; a program needn't handle non-finite values.
Results may differ from a plain program's by a relative error of at most 0.0034.
Values may be sent and summed in bfloat16 or wider, within the bound.
No kernel may reach another device: no remote copies, remote signals or barrier semaphores. Data moves between devices by JAX's collectives and lax.ppermute only.
A program may use at most 64 MiB of HBM per device.

v0:
```python
import math
import jax
import jax.numpy as jnp
from jax import lax
from jax.sharding import PartitionSpec as P

L = 256
BLK = 128
PB = 512
learn_rate = 1.0
phase_shift = 0.1


def dft_tables():
    freq_ids = jnp.arange(L, dtype=jnp.int32)
    product = (freq_ids[:, None] - L // 2) * freq_ids[None, :] % L
    angle = 2.0 * math.pi / L * product.astype(jnp.float32)
    return (jnp.cos(angle).astype(jnp.bfloat16), jnp.sin(angle).astype(jnp.bfloat16))


def transform(pictures, cos_table, sin_table):
    row_cos = jnp.einsum(
        "iyx,kx->iyk", pictures, cos_table, preferred_element_type=jnp.float32
    ).astype(jnp.bfloat16)
    row_sin = jnp.einsum(
        "iyx,kx->iyk", pictures, sin_table, preferred_element_type=jnp.float32
    ).astype(jnp.bfloat16)
    real_part = (
        jnp.einsum("ay,iyb->iab", cos_table, row_cos, preferred_element_type=jnp.float32)
        - jnp.einsum("ay,iyb->iab", sin_table, row_sin, preferred_element_type=jnp.float32)
    ) / L
    imag_part = (
        -(
            jnp.einsum("ay,iyb->iab", sin_table, row_cos, preferred_element_type=jnp.float32)
            + jnp.einsum("ay,iyb->iab", cos_table, row_sin, preferred_element_type=jnp.float32)
        )
        / L
    )
    count_img = pictures.shape[0]
    blocks = jnp.concatenate(
        [real_part.reshape(count_img, PB, BLK), imag_part.reshape(count_img, PB, BLK)], axis=2
    )
    return blocks.reshape(count_img * PB, 2 * BLK).astype(jnp.bfloat16)


def ctf_rows(pixel_ids, focus):
    block_id = pixel_ids % PB
    row_id = block_id // (L // BLK)
    col_id = block_id % (L // BLK) * BLK
    lane_ids = jnp.arange(BLK, dtype=jnp.int32)
    freq_y = (row_id - L // 2).astype(jnp.float32) / L
    freq_x = (col_id[..., None] + lane_ids - L // 2).astype(jnp.float32) / L
    radius = freq_x * freq_x + (freq_y * freq_y)[..., None]
    return -jnp.sin(math.pi * focus.astype(jnp.float32)[..., None] * radius + phase_shift)


def residual_terms(prediction, observed, ctf_values, live_slots):
    shape = prediction.shape
    pred_wide = prediction.astype(jnp.float32).reshape(shape[:-1] + (2, BLK))
    obs_wide = observed.astype(jnp.float32).reshape(shape[:-1] + (2, BLK))
    factor = ctf_values[..., None, :]
    misfit = factor * (factor * pred_wide - obs_wide)
    misfit = jnp.where(live_slots[..., None, None], misfit, 0.0)
    return misfit.reshape(shape).astype(jnp.bfloat16)


def tap_matrix(tap_ids, weights, block_count):
    owners, taps, slots = tap_ids.shape
    flat_taps = jnp.transpose(tap_ids, (0, 2, 1)).reshape(owners * slots, taps)
    flat_weights = jnp.transpose(weights, (0, 2, 1)).reshape(owners * slots, taps)
    block_ids = jnp.arange(block_count, dtype=jnp.int32)
    picked = jnp.where(
        flat_taps[:, :, None] == block_ids[None, None, :],
        flat_weights[:, :, None],
        jnp.zeros((), jnp.bfloat16),
    )
    return jnp.sum(picked, axis=1, dtype=jnp.bfloat16)


def predict_rows(matrix, extract, owners):
    summed = jnp.dot(matrix, extract, preferred_element_type=jnp.float32)
    return summed.reshape(owners, -1, extract.shape[1])


def local(images, defocus, volume, counts, slot_pixel, slot_taps, slot_weights):
    cos_table, sin_table = dft_tables()
    extract = volume.astype(jnp.bfloat16)
    slot_count = counts[0, 0]
    pixel_ids = slot_pixel[0, 0]
    tap_ids = slot_taps[0, 0]
    weights = slot_weights[0, 0]
    owners = pixel_ids.shape[0]
    capacity = pixel_ids.shape[1]
    live_slots = jnp.arange(capacity, dtype=jnp.int32)[None, :] < slot_count[:, None]
    got_taps, got_weights = (
        lax.all_to_all(tap_ids, "vol", split_axis=0, concat_axis=0, tiled=True),
        lax.all_to_all(weights, "vol", split_axis=0, concat_axis=0, tiled=True),
    )
    matrix = tap_matrix(got_taps, got_weights, volume.shape[0])
    prediction = predict_rows(matrix, extract, owners).astype(jnp.bfloat16)
    returned = lax.all_to_all(prediction, "vol", split_axis=0, concat_axis=0, tiled=True)
    observed = transform(images, cos_table, sin_table)
    ctf_values = ctf_rows(pixel_ids, defocus[pixel_ids // PB])
    weighted = residual_terms(returned, observed[pixel_ids], ctf_values, live_slots)
    got_residual = lax.all_to_all(weighted, "vol", split_axis=0, concat_axis=0, tiled=True)
    flat_residual = got_residual.reshape(-1, volume.shape[1])
    gradient = lax.dot_general(
        matrix, flat_residual, (((0,), (0,)), ((), ())), preferred_element_type=jnp.float32
    )
    gradient = lax.psum(gradient, "ptcl")
    return volume - learn_rate * gradient


def solution(mesh):
    placed = (
        P(("vol", "ptcl"), None, None),
        P(("vol", "ptcl")),
        P("vol", None),
        P("vol", "ptcl", None),
        P("vol", "ptcl", None, None),
        P("vol", "ptcl", None, None, None),
        P("vol", "ptcl", None, None, None),
    )
    return jax.shard_map(
        local, mesh=mesh, in_specs=placed, out_specs=P("vol", None), check_vma=False
    )
```

profile of v0, /device:TPU:0, one launch (start us, length us, event | category | flops | bytes accessed | tf_op | source)
XLA Modules:
  0.0 113.2 jit_solution(16446139586523251480)
XLA Ops:
  6.5 7.4 %all-to-all-start.1 = ((bf16[8,8,96]{2,1,0:T(8,128)(2,1)}), bf16[8,8,96]{2,1,0:T(8,128)(2,1)S(1)}, u32[]{:S(2)}, u32[]{:S(2)}) async-start(bf16[8,8,96]{2,1,0:T(8,128)(2,1)} %bitcast.56), calls=%async_computation.1 | async-start | bytes 32768 | tf_op jit(solution)/shard_map/all_to_all | solution.py:97
  14.0 0.7 fusion.29
  14.7 0.7 fusion.25
  15.4 1.1 %convolution_convert_fusion.2 = bf16[256,256]{1,0:T(8,128)(2,1)S(1)} fusion(bf16[1,256,256]{2,1,0:T(8,128)(2,1)S(1)} %copy-done, s32[256]{0:T(256)S(1)} %iota_add_fusion), kind=kOutput, calls=%fused_computation.13 | convolution fusion | flops 34603008 | bytes 263168 | tf_op jit(solution)/shard_map/iyx,kx->iyk/dot_general | solution.py:22
  16.5 1.2 %fusion.23 = f32[256,256]{1,0:T(8,128)S(1)} fusion(bf16[256,256]{1,0:T(8,128)(2,1)S(1)} %convolution_convert_fusion.2, s32[256]{0:T(256)S(1)} %iota_add_fusion), kind=kOutput, calls=%fused_computation.38 | convolution fusion | flops 34537472 | bytes 394240 | tf_op jit(solution)/shard_map/ay,iyb->iab/dot_general | solution.py:34
  17.7 1.2 %fusion.22 = f32[256,256]{1,0:T(8,128)S(1)} fusion(bf16[256,256]{1,0:T(8,128)(2,1)S(1)} %convolution_convert_fusion.2, s32[256]{0:T(256)S(1)} %iota_add_fusion), kind=kOutput, calls=%fused_computation.37 | convolution fusion | flops 34537472 | bytes 394240 | tf_op jit(solution)/shard_map/ay,iyb->iab/dot_general | solution.py:29
  19.6 1.5 %sine_negate_fusion = f32[8,96,128]{2,1,0:T(8,128)S(1)} fusion(f32[8,96]{1,0:T(8,128)S(1)} %fusion.29, s32[8,96]{1,0:T(8,128)S(1)} %fusion.25, f32[]{:T(128)} %bitcast.7), kind=kLoop, calls=%fused_computation.23 | loop fusion | flops 884736 | bytes 399364 | tf_op jit(solution)/shard_map/neg | solution.py:54
  21.1 1.2 %convolution_convert_fusion.1 = bf16[256,256]{1,0:T(8,128)(2,1)S(1)} fusion(bf16[1,256,256]{2,1,0:T(8,128)(2,1)S(1)} %copy-done, s32[256]{0:T(256)S(1)} %iota_add_fusion), kind=kOutput, calls=%fused_computation.12 | convolution fusion | flops 34603008 | bytes 263168 | tf_op jit(solution)/shard_map/iyx,kx->iyk/dot_general | solution.py:25
  22.2 6.0 %all-to-all-start = ((s32[8,8,96]{2,1,0:T(8,128)}), s32[8,8,96]{2,1,0:T(8,128)S(1)}, u32[]{:S(2)}, u32[]{:S(2)}) async-start(s32[8,8,96]{2,1,0:T(8,128)} %bitcast), calls=%async_computation | async-start | bytes 65536 | tf_op jit(solution)/shard_map/all_to_all | solution.py:96
  28.2 1.2 %fusion.7 = bf16[1,256,256]{1,2,0:T(8,128)(2,1)S(1)} fusion(f32[256,256]{1,0:T(8,128)S(1)} %fusion.23, bf16[256,256]{1,0:T(8,128)(2,1)S(1)} %convolution_convert_fusion.1, s32[256]{0:T(256)S(1)} %iota_add_fusion), kind=kOutput, calls=%fused_computation.14 | convolution fusion | flops 34799616 | bytes 525312 | tf_op jit(solution)/shard_map/ay,iyb->iab/dot_general | solution.py:35
  29.6 5.3 %all-to-all-done = s32[8,8,96]{2,1,0:T(8,128)S(1)} async-done(((s32[8,8,96]{2,1,0:T(8,128)}), s32[8,8,96]{2,1,0:T(8,128)S(1)}, u32[]{:S(2)}, u32[]{:S(2)}) %all-to-all-start) | async-done | bytes 24608 | tf_op jit(solution)/shard_map/all_to_all | solution.py:96
  35.1 5.1 %fusion.1 = bf16[768,512]{1,0:T(8,128)(2,1)S(1)} fusion(s32[768,8]{1,0:T(8,128)S(1)} %bitcast.51, bf16[768,8]{1,0:T(8,128)(2,1)S(1)} %bitcast.52), kind=kLoop, calls=%fused_computation.3 | loop fusion | flops 9043968 | bytes 823296 | tf_op jit(solution)/shard_map/reduce_sum | solution.py:77
  40.2 1.1 convolution_convert_fusion
  41.3 4.1 %all-to-all-start.2 = ((bf16[8,96,256]{2,1,0:T(8,128)(2,1)}), bf16[8,96,256]{2,1,0:T(8,128)(2,1)}, u32[]{:S(2)}, u32[]{:S(2)}) async-start(bf16[8,96,256]{2,1,0:T(8,128)(2,1)} %convolution_convert_fusion), calls=%async_computation.2 | async-start | bytes 786432 | tf_op jit(solution)/shard_map/all_to_all | solution.py:101
  45.6 1.2 %fusion.8 = bf16[1,256,256]{1,2,0:T(8,128)(2,1)S(1)} fusion(f32[256,256]{1,0:T(8,128)S(1)} %fusion.22, bf16[256,256]{1,0:T(8,128)(2,1)S(1)} %convolution_convert_fusion.1, s32[256]{0:T(256)S(1)} %iota_add_fusion), kind=kOutput, calls=%fused_computation.15 | convolution fusion | flops 34734080 | bytes 525312 | tf_op jit(solution)/shard_map/ay,iyb->iab/dot_general | solution.py:30
  47.1 0.6 mul.128
  48.1 0.4 copy-done.2
  48.6 2.7 %gather_fusion = bf16[768,256]{1,0:T(8,128)(2,1)S(1)} fusion(bf16[512,256]{1,0:T(8,128)(2,1)S(1)} %maximum_bitcast_fusion, s32[1024]{0:T(1024)S(1)} %pad_clamp_fusion), kind=kCustom, calls=%fused_computation | custom fusion | bytes 789504 | tf_op jit(solution)/shard_map/gather | solution.py:104
  51.3 4.0 %all-to-all-done.2 = bf16[8,96,256]{2,1,0:T(8,128)(2,1)} async-done(((bf16[8,96,256]{2,1,0:T(8,128)(2,1)}), bf16[8,96,256]{2,1,0:T(8,128)(2,1)}, u32[]{:S(2)}, u32[]{:S(2)}) %all-to-all-start.2) | async-done | bytes 393248 | tf_op jit(solution)/shard_map/all_to_all | solution.py:101
  55.4 1.2 %fusion.11 = bf16[8,96,256]{2,1,0:T(8,128)(2,1)S(1)} fusion(f32[8,96,256]{2,1,0:T(8,128)S(1)} %mul.128, bf16[8,96,256]{2,1,0:T(8,128)(2,1)S(1)} %bitcast.50, bf16[8,96,256]{2,1,0:T(8,128)(2,1)} %all-to-all-done.2, pred[8,96]{1,0:T(8,128)(4,1)S(1)} %iota_compare_fusion.1), kind=kLoop, calls=%fused_computation.19 | loop fusion | flops 1376256 | bytes 1966848 | tf_op jit(solution)/shard_map/convert_element_type | solution.py:64
  56.6 14.6 %all_to_all.20 = bf16[8,96,256]{2,1,0:T(8,128)(2,1)S(1)} all-to-all(bf16[8,96,256]{2,1,0:T(8,128)(2,1)S(1)} %fusion.11), channel_id=1, replica_groups=mesh['vol'=8,'ptcl'=4] {'vol'}, dimensions={0} | all-to-all | bytes 786432 | tf_op jit(solution)/shard_map/all_to_all | solution.py:105
  71.2 1.2 %fusion.56 = f32[512,256]{1,0:T(8,128)} fusion(bf16[768,512]{1,0:T(8,128)(2,1)S(1)} %fusion.1, bf16[768,256]{1,0:T(8,128)(2,1)S(1)} %bitcast.53), kind=kOutput, calls=%fused_computation.84 | convolution fusion | flops 201326592 | bytes 1703936 | tf_op jit(solution)/shard_map/dot_general | solution.py:107
  72.4 32.0 %all-reduce.2.cloned.1.call-done = f32[512,256]{1,0:T(8,128)} async-done(((f32[512,256]{1,0:T(8,128)}), f32[512,256]{1,0:T(8,128)}) %all-reduce.2.cloned.1.call-update) | async-done | bytes 524304 | tf_op jit(solution)/shard_map/psum | solution.py:110
  104.4 1.9 %sub.47 = f32[512,256]{1,0:T(8,128)} subtract(f32[512,256]{1,0:T(8,128)S(1)} %copy-done.1, f32[512,256]{1,0:T(8,128)} %all-reduce.2.cloned.1.call-done) | non-fusion elementwise | flops 131072 | bytes 1572864 | tf_op jit(solution)/shard_map/sub | solution.py:111
  (23 shorter events, 1.3 us)
Async XLA Ops:
  6.5 8.8 %copy-start = (bf16[1,256,256]{2,1,0:T(8,128)(2,1)S(1)}, bf16[1,256,256]{2,1,0:T(8,128)(2,1)}, u32[]{:S(2)}) copy-start(bf16[1,256,256]{2,1,0:T(8,128)(2,1)} %param.7) | copy-start | bytes 393220
  6.5 15.7 %all-to-all-start.1 = ((bf16[8,8,96]{2,1,0:T(8,128)(2,1)}), bf16[8,8,96]{2,1,0:T(8,128)(2,1)S(1)}, u32[]{:S(2)}, u32[]{:S(2)}) async-start(bf16[8,8,96]{2,1,0:T(8,128)(2,1)} %bitcast.56), calls=%async_computation.1 | async-start | bytes 32768 | tf_op jit(solution)/shard_map/all_to_all | solution.py:97
  22.2 12.7 %all-to-all-start = ((s32[8,8,96]{2,1,0:T(8,128)}), s32[8,8,96]{2,1,0:T(8,128)S(1)}, u32[]{:S(2)}, u32[]{:S(2)}) async-start(s32[8,8,96]{2,1,0:T(8,128)} %bitcast), calls=%async_computation | async-start | bytes 65536 | tf_op jit(solution)/shard_map/all_to_all | solution.py:96
  35.1 5.1 %copy-start.1 = (f32[512,256]{1,0:T(8,128)S(1)}, f32[512,256]{1,0:T(8,128)}, u32[]{:S(2)}) copy-start(f32[512,256]{1,0:T(8,128)} %param.9) | copy-start | bytes 1572868
  41.3 14.1 %all-to-all-start.2 = ((bf16[8,96,256]{2,1,0:T(8,128)(2,1)}), bf16[8,96,256]{2,1,0:T(8,128)(2,1)}, u32[]{:S(2)}, u32[]{:S(2)}) async-start(bf16[8,96,256]{2,1,0:T(8,128)(2,1)} %convolution_convert_fusion), calls=%async_computation.2 | async-start | bytes 786432 | tf_op jit(solution)/shard_map/all_to_all | solution.py:101
  45.4 59.0 %all-reduce.2.cloned.1.call-start = ((), (), s32[]{:S(2)}) async-start(), calls=%async_computation.4 | async-start | bytes 1048576 | tf_op jit(solution)/shard_map/psum | solution.py:110
  47.8 0.7 copy-start.2
  48.6 2.7 %copy-start.3 = (s32[1,1,8]{2,1,0:T(1,128)S(1)}, s32[1,1,8]{2,1,0:T(1,128)}, u32[]{:S(2)}) copy-start(s32[1,1,8]{2,1,0:T(1,128)} %param.10) | copy-start | bytes 100
Sparse Core Ops, SparseCore 0:
  72.5 31.8 all-reduce.1
where the time goes:
time: 114 us; the launch traced here: 113 us
  waiting for transfers between devices  41.4 us (36%)
  starting transfers between devices  17.7 us (16%)
  blocking collectives  14.6 us (13%)
  between operations  14.2 us (12%)
  other arithmetic  11.1 us (10%)
  matrix products  9.4 us (8%)
  local copies, waits for them, and re-layouts  4.61 us (4%)
    psum x1, waiting for transfers between devices, local(): gradient = lax.psum(gradient, 'ptcl')  32 us
    all_to_all x1, blocking collectives, local(): lax.all_to_all(weighted, 'vol', split_axis=0, concat_axis=0, tiled=True)  14.6 us
    all_to_all x1, starting transfers between devices, local(): lax.all_to_all(weights, 'vol', split_axis=0, concat_axis=0, tiled=True)  7.41 us
    all_to_all x1, starting transfers between devices, local(): lax.all_to_all(tap_ids, 'vol', split_axis=0, concat_axis=0, tiled=True)  6.01 us
    all_to_all x1, waiting for transfers between devices, local(): lax.all_to_all(tap_ids, 'vol', split_axis=0, concat_axis=0, tiled=True)  5.34 us
    reduce_sum x1, other arithmetic, tap_matrix(): return jnp.sum(picked, axis=1, dtype=jnp.bfloat16)  5.06 us
    all_to_all x1, starting transfers between devices, local(): lax.all_to_all(prediction, 'vol', split_axis=0, concat_axis=0, tiled=True)  4.09 us
    all_to_all x1, waiting for transfers between devices, local(): lax.all_to_all(prediction, 'vol', split_axis=0, concat_axis=0, tiled=True)  4.04 us
  transfers between devices with their start and end apart: 4, of which 3 were waited for; matrix products, arithmetic and copies ran while one was open for 13% of the time, Pallas kernels for 0%

commit v1 on v0

--- a/solution.py
+++ b/solution.py
@@ -107,7 +107,7 @@
     gradient = lax.dot_general(
         matrix, flat_residual, (((0,), (0,)), ((), ())), preferred_element_type=jnp.float32
     )
-    gradient = lax.psum(gradient, "ptcl")
+    gradient = jnp.sum(lax.all_gather(gradient, "ptcl"), axis=0)
     return volume - learn_rate * gradient
 
 

time: 114 us -> 104 us (0.912)
  waiting for transfers between devices: 41.4 us -> 31.1 us
    psum x1 -> x0, waiting for transfers between devices: 32 us -> none  [local(): gradient = lax.psum(gradient, 'ptcl')]
    all_gather x0 -> x1, waiting for transfers between devices: none -> 21.4 us  [local(): gradient = jnp.sum(lax.all_gather(gradient, 'ptcl'), axis=0)]
    reduce_sum x0 -> x1, other arithmetic: none -> 1.79 us  [local(): gradient = jnp.sum(lax.all_gather(gradient, 'ptcl'), axis=0)]
  transfers between devices with their start and end apart: 4 -> 4, of which waited for: 3 -> 3; matrix products, arithmetic and copies ran while one was open for 13% -> 14% of each run, Pallas kernels for 0% -> 0%
where the time goes in v1:
time: 104 us; the launch traced here: 103 us
  waiting for transfers between devices  31.1 us (30%)
  starting transfers between devices  17.7 us (17%)
  blocking collectives  14.6 us (14%)
  between operations  14.3 us (14%)
  other arithmetic  11.9 us (11%)
  matrix products  9.4 us (9%)
  local copies, waits for them, and re-layouts  4.25 us (4%)
    all_gather x1, waiting for transfers between devices, local(): gradient = jnp.sum(lax.all_gather(gradient, 'ptcl'), axis=0)  21.4 us
    all_to_all x1, blocking collectives, local(): lax.all_to_all(weighted, 'vol', split_axis=0, concat_axis=0, tiled=True)  14.6 us
    all_to_all x1, starting transfers between devices, local(): lax.all_to_all(weights, 'vol', split_axis=0, concat_axis=0, tiled=True)  7.41 us
    all_to_all x1, starting transfers between devices, local(): lax.all_to_all(tap_ids, 'vol', split_axis=0, concat_axis=0, tiled=True)  6.01 us
    all_to_all x1, waiting for transfers between devices, local(): lax.all_to_all(tap_ids, 'vol', split_axis=0, concat_axis=0, tiled=True)  5.34 us
    reduce_sum x1, other arithmetic, tap_matrix(): return jnp.sum(picked, axis=1, dtype=jnp.bfloat16)  5.06 us
    all_to_all x1, waiting for transfers between devices, local(): lax.all_to_all(prediction, 'vol', split_axis=0, concat_axis=0, tiled=True)  4.38 us
    all_to_all x1, starting transfers between devices, local(): lax.all_to_all(prediction, 'vol', split_axis=0, concat_axis=0, tiled=True)  4.09 us
  transfers between devices with their start and end apart: 4, of which 3 were waited for; matrix products, arithmetic and copies ran while one was open for 14% of the time, Pallas kernels for 0%

profile of v1, /device:TPU:0, one launch (start us, length us, event | category | flops | bytes accessed | tf_op | source)
XLA Modules:
  0.0 103.3 jit_solution(8349849920351582564)
XLA Ops:
  6.5 7.4 %all-to-all-start.1 = ((bf16[8,8,96]{2,1,0:T(8,128)(2,1)}), bf16[8,8,96]{2,1,0:T(8,128)(2,1)S(1)}, u32[]{:S(2)}, u32[]{:S(2)}) async-start(bf16[8,8,96]{2,1,0:T(8,128)(2,1)} %bitcast.58), calls=%async_computation.1 | async-start | bytes 32768 | tf_op jit(solution)/shard_map/all_to_all | solution.py:97
  14.0 0.7 fusion.29
  14.7 0.7 fusion.25
  15.4 1.1 %convolution_convert_fusion.2 = bf16[256,256]{1,0:T(8,128)(2,1)S(1)} fusion(bf16[1,256,256]{2,1,0:T(8,128)(2,1)S(1)} %copy-done, s32[256]{0:T(256)S(1)} %iota_add_fusion), kind=kOutput, calls=%fused_computation.13 | convolution fusion | flops 34603008 | bytes 263168 | tf_op jit(solution)/shard_map/iyx,kx->iyk/dot_general | solution.py:22
  16.5 1.2 %fusion.23 = f32[256,256]{1,0:T(8,128)S(1)} fusion(bf16[256,256]{1,0:T(8,128)(2,1)S(1)} %convolution_convert_fusion.2, s32[256]{0:T(256)S(1)} %iota_add_fusion), kind=kOutput, calls=%fused_computation.38 | convolution fusion | flops 34537472 | bytes 394240 | tf_op jit(solution)/shard_map/ay,iyb->iab/dot_general | solution.py:34
  17.7 1.2 %fusion.22 = f32[256,256]{1,0:T(8,128)S(1)} fusion(bf16[256,256]{1,0:T(8,128)(2,1)S(1)} %convolution_convert_fusion.2, s32[256]{0:T(256)S(1)} %iota_add_fusion), kind=kOutput, calls=%fused_computation.37 | convolution fusion | flops 34537472 | bytes 394240 | tf_op jit(solution)/shard_map/ay,iyb->iab/dot_general | solution.py:29
  19.6 1.5 %sine_negate_fusion = f32[8,96,128]{2,1,0:T(8,128)S(1)} fusion(f32[8,96]{1,0:T(8,128)S(1)} %fusion.29, s32[8,96]{1,0:T(8,128)S(1)} %fusion.25, f32[]{:T(128)} %bitcast.7), kind=kLoop, calls=%fused_computation.23 | loop fusion | flops 884736 | bytes 399364 | tf_op jit(solution)/shard_map/neg | solution.py:54
  21.1 1.2 %convolution_convert_fusion.1 = bf16[256,256]{1,0:T(8,128)(2,1)S(1)} fusion(bf16[1,256,256]{2,1,0:T(8,128)(2,1)S(1)} %copy-done, s32[256]{0:T(256)S(1)} %iota_add_fusion), kind=kOutput, calls=%fused_computation.12 | convolution fusion | flops 34603008 | bytes 263168 | tf_op jit(solution)/shard_map/iyx,kx->iyk/dot_general | solution.py:25
  22.2 6.0 %all-to-all-start = ((s32[8,8,96]{2,1,0:T(8,128)}), s32[8,8,96]{2,1,0:T(8,128)S(1)}, u32[]{:S(2)}, u32[]{:S(2)}) async-start(s32[8,8,96]{2,1,0:T(8,128)} %bitcast), calls=%async_computation | async-start | bytes 65536 | tf_op jit(solution)/shard_map/all_to_all | solution.py:96
  28.3 1.2 %fusion.7 = bf16[1,256,256]{1,2,0:T(8,128)(2,1)S(1)} fusion(f32[256,256]{1,0:T(8,128)S(1)} %fusion.23, bf16[256,256]{1,0:T(8,128)(2,1)S(1)} %convolution_convert_fusion.1, s32[256]{0:T(256)S(1)} %iota_add_fusion), kind=kOutput, calls=%fused_computation.14 | convolution fusion | flops 34799616 | bytes 525312 | tf_op jit(solution)/shard_map/ay,iyb->iab/dot_general | solution.py:35
  29.6 5.3 %all-to-all-done = s32[8,8,96]{2,1,0:T(8,128)S(1)} async-done(((s32[8,8,96]{2,1,0:T(8,128)}), s32[8,8,96]{2,1,0:T(8,128)S(1)}, u32[]{:S(2)}, u32[]{:S(2)}) %all-to-all-start) | async-done | bytes 24608 | tf_op jit(solution)/shard_map/all_to_all | solution.py:96
  35.1 5.1 %fusion.1 = bf16[768,512]{1,0:T(8,128)(2,1)S(1)} fusion(s32[768,8]{1,0:T(8,128)S(1)} %bitcast.53, bf16[768,8]{1,0:T(8,128)(2,1)S(1)} %bitcast.54), kind=kLoop, calls=%fused_computation.3 | loop fusion | flops 9043968 | bytes 823296 | tf_op jit(solution)/shard_map/reduce_sum | solution.py:77
  40.2 1.1 %convolution_convert_fusion = bf16[8,96,256]{2,1,0:T(8,128)(2,1)} fusion(bf16[8,96,512]{2,1,0:T(8,128)(2,1)S(1)} %bitcast.50, f32[512,256]{1,0:T(8,128)S(1)} %copy-done.1), kind=kOutput, calls=%fused_computation.4 | convolution fusion | flops 201654272 | bytes 1703936 | tf_op jit(solution)/shard_map/dot_general | solution.py:81
  41.3 4.1 %all-to-all-start.2 = ((bf16[8,96,256]{2,1,0:T(8,128)(2,1)}), bf16[8,96,256]{2,1,0:T(8,128)(2,1)}, u32[]{:S(2)}, u32[]{:S(2)}) async-start(bf16[8,96,256]{2,1,0:T(8,128)(2,1)} %convolution_convert_fusion), calls=%async_computation.2 | async-start | bytes 786432 | tf_op jit(solution)/shard_map/all_to_all | solution.py:101
  45.6 1.2 %fusion.8 = bf16[1,256,256]{1,2,0:T(8,128)(2,1)S(1)} fusion(f32[256,256]{1,0:T(8,128)S(1)} %fusion.22, bf16[256,256]{1,0:T(8,128)(2,1)S(1)} %convolution_convert_fusion.1, s32[256]{0:T(256)S(1)} %iota_add_fusion), kind=kOutput, calls=%fused_computation.15 | convolution fusion | flops 34734080 | bytes 525312 | tf_op jit(solution)/shard_map/ay,iyb->iab/dot_general | solution.py:30
  47.1 0.6 mul.128
  48.2 2.7 %gather_fusion = bf16[768,256]{1,0:T(8,128)(2,1)S(1)} fusion(bf16[512,256]{1,0:T(8,128)(2,1)S(1)} %maximum_bitcast_fusion, s32[1024]{0:T(1024)S(1)} %pad_clamp_fusion), kind=kCustom, calls=%fused_computation | custom fusion | bytes 789504 | tf_op jit(solution)/shard_map/gather | solution.py:104
  51.0 4.4 %all-to-all-done.2 = bf16[8,96,256]{2,1,0:T(8,128)(2,1)} async-done(((bf16[8,96,256]{2,1,0:T(8,128)(2,1)}), bf16[8,96,256]{2,1,0:T(8,128)(2,1)}, u32[]{:S(2)}, u32[]{:S(2)}) %all-to-all-start.2) | async-done | bytes 393248 | tf_op jit(solution)/shard_map/all_to_all | solution.py:101
  55.4 1.2 %fusion.11 = bf16[8,96,256]{2,1,0:T(8,128)(2,1)S(1)} fusion(f32[8,96,256]{2,1,0:T(8,128)S(1)} %mul.128, bf16[8,96,256]{2,1,0:T(8,128)(2,1)S(1)} %bitcast.52, bf16[8,96,256]{2,1,0:T(8,128)(2,1)} %all-to-all-done.2, pred[8,96]{1,0:T(8,128)(4,1)S(1)} %iota_compare_fusion.1), kind=kLoop, calls=%fused_computation.19 | loop fusion | flops 1376256 | bytes 1966848 | tf_op jit(solution)/shard_map/convert_element_type | solution.py:64
  56.6 14.6 %all_to_all.20 = bf16[8,96,256]{2,1,0:T(8,128)(2,1)S(1)} all-to-all(bf16[8,96,256]{2,1,0:T(8,128)(2,1)S(1)} %fusion.11), channel_id=1, replica_groups=mesh['vol'=8,'ptcl'=4] {'vol'}, dimensions={0} | all-to-all | bytes 786432 | tf_op jit(solution)/shard_map/all_to_all | solution.py:105
  71.2 1.2 %fusion.56 = f32[512,256]{1,0:T(8,128)} fusion(bf16[768,512]{1,0:T(8,128)(2,1)S(1)} %fusion.1, bf16[768,256]{1,0:T(8,128)(2,1)S(1)} %bitcast.55), kind=kOutput, calls=%fused_computation.84 | convolution fusion | flops 201326592 | bytes 1703936 | tf_op jit(solution)/shard_map/dot_general | solution.py:107
  72.4 21.4 %all-gather.3.cloned.1.call-done = f32[2048,256]{1,0:T(8,128)} async-done(((f32[512,256]{1,0:T(8,128)}), f32[2048,256]{1,0:T(8,128)}) %all-gather.3.cloned.1.call-update) | async-done | bytes 2097168 | tf_op jit(solution)/shard_map/all_gather | solution.py:110
  93.8 1.8 %reduce_sum.19 = f32[512,256]{1,0:T(8,128)S(1)} reduce(f32[4,512,256]{2,1,0:T(8,128)} %bitcast.51, f32[]{:T(128)} %constant.86.clone.1), dimensions={0}, to_apply=%region_1.2 | reduce | flops 393216 | bytes 2621444 | tf_op jit(solution)/shard_map/reduce_sum | solution.py:110
  95.6 0.9 sub.47
  (24 shorter events, 1.3 us)
Async XLA Ops:
  6.5 8.8 %copy-start = (bf16[1,256,256]{2,1,0:T(8,128)(2,1)S(1)}, bf16[1,256,256]{2,1,0:T(8,128)(2,1)}, u32[]{:S(2)}) copy-start(bf16[1,256,256]{2,1,0:T(8,128)(2,1)} %param.7) | copy-start | bytes 393220
  6.5 15.7 %all-to-all-start.1 = ((bf16[8,8,96]{2,1,0:T(8,128)(2,1)}), bf16[8,8,96]{2,1,0:T(8,128)(2,1)S(1)}, u32[]{:S(2)}, u32[]{:S(2)}) async-start(bf16[8,8,96]{2,1,0:T(8,128)(2,1)} %bitcast.58), calls=%async_computation.1 | async-start | bytes 32768 | tf_op jit(solution)/shard_map/all_to_all | solution.py:97
  21.1 19.1 %copy-start.1 = (f32[512,256]{1,0:T(8,128)S(1)}, f32[512,256]{1,0:T(8,128)}, u32[]{:S(2)}) copy-start(f32[512,256]{1,0:T(8,128)} %param.9) | copy-start | bytes 1572868
  22.2 12.7 %all-to-all-start = ((s32[8,8,96]{2,1,0:T(8,128)}), s32[8,8,96]{2,1,0:T(8,128)S(1)}, u32[]{:S(2)}, u32[]{:S(2)}) async-start(s32[8,8,96]{2,1,0:T(8,128)} %bitcast), calls=%async_computation | async-start | bytes 65536 | tf_op jit(solution)/shard_map/all_to_all | solution.py:96
  41.3 14.1 %all-to-all-start.2 = ((bf16[8,96,256]{2,1,0:T(8,128)(2,1)}), bf16[8,96,256]{2,1,0:T(8,128)(2,1)}, u32[]{:S(2)}, u32[]{:S(2)}) async-start(bf16[8,96,256]{2,1,0:T(8,128)(2,1)} %convolution_convert_fusion), calls=%async_computation.2 | async-start | bytes 786432 | tf_op jit(solution)/shard_map/all_to_all | solution.py:101
  45.4 48.4 %all-gather.3.cloned.1.call-start = ((), (), s32[]{:S(2)}) async-start(), calls=%async_computation.4 | async-start | bytes 2621440 | tf_op jit(solution)/shard_map/all_gather | solution.py:110
  46.8 1.3 %copy-start.2 = (s32[1,1,8,96]{3,2,1,0:T(8,128)S(1)}, s32[1,1,8,96]{3,2,1,0:T(8,128)}, u32[]{:S(2)}) copy-start(s32[1,1,8,96]{3,2,1,0:T(8,128)} %param.11) | copy-start | bytes 9220
  48.1 2.8 %copy-start.3 = (s32[1,1,8]{2,1,0:T(1,128)S(1)}, s32[1,1,8]{2,1,0:T(1,128)}, u32[]{:S(2)}) copy-start(s32[1,1,8]{2,1,0:T(1,128)} %param.10) | copy-start | bytes 100
Sparse Core Ops, SparseCore 0:
  72.5 21.2 all-gather.2
